TPU v7x, 512 devices: a whole 4x8x8 slice. The times are simulated.
512 devices in a mesh: seg: 16 (over z, x_lo), tok: 32 (over x_hi, y, core).
Axes of the slice: x: 4 (x_hi: 2, x_lo: 2; x = x_hi * 2 + x_lo), y: 8, z: 8, core: 2. Of those that a mesh axis runs over, the one named last changes fastest.
Arguments:
- seg_queries: bfloat16 [16, 4096, 2048], P('seg', 'tok'), may hold values from -8 to 8
- seg_keys: bfloat16 [16, 4096, 512], P('seg', 'tok'), may hold values from -8 to 8
- seg_values: bfloat16 [16, 4096, 512], P('seg', 'tok'), may hold values from -8 to 8
- grad_out: bfloat16 [16, 4096, 2048], P('seg', 'tok'), may hold values from -6 to 6
- mem_init: float32 [256, 1024], P('tok'), may hold values from -6 to 6
- mem_query: bfloat16 [256, 512], P('tok'), may hold values from -8 to 8
- retention: float32 [16, 1024], P('seg'), may hold values from 0 to 1
- seg_len: int32 [16], replicated, may hold values from 1024 to 4096, as said below
- doc_start: int32 [16], replicated, may hold values from 0 to 1, as said below
Outputs:
- attended: bfloat16 [16, 4096, 2048], P('seg', 'tok')
- memory_in: float32 [16, 256, 1024], P('seg', 'tok')
- memory_grad: float32 [16, 256, 1024], P('seg', 'tok')
Inputs may be any that keep to these rules, and one draw needn't show every extreme that they name: `seg_len`: A segment is full unless it is the last one of its document; segment 0 is always full and the last segment is the last one of its document. `doc_start`: segment 0 begins a document and segment 1 never does; any later segment may.
All inputs are finite; a program needn't handle non-finite values.
Results may differ from a plain program's by a relative error of at most 0.009.
Values may be sent and summed in bfloat16 or wider, within the bound.
No kernel may reach another device: no remote copies, remote signals or barrier semaphores. Data moves between devices by JAX's collectives and lax.ppermute only.
A program may use at most 64 MiB of HBM per device.

v0:
```python
import math
import jax
import jax.numpy as jnp
from jax import lax
from jax.sharding import PartitionSpec as P

HD = 128
QH = 16
KVH = 4
loss_scale = 16.0
neg_fill = -1e30
norm_eps = 1e-06


def gathered(block, axis, groups):
    size = lax.axis_size(axis)
    index = lax.axis_index(axis)
    held = block[None]
    axis_bits = []
    for group in groups:
        group = sorted(group)
        mine = sum(((index >> bit & 1) << k for k, bit in enumerate(group)))
        arrived = [held]
        for mask in range(1, 1 << len(group)):
            flip = sum(((mask >> k & 1) << bit for k, bit in enumerate(group)))
            arrived.append(lax.ppermute(held, axis, [(i, i ^ flip) for i in range(size)]))
        placed = []
        for place in range(1 << len(group)):
            value = arrived[0]
            for mask in range(1, 1 << len(group)):
                value = jnp.where(mine ^ mask == place, arrived[mask], value)
            placed.append(value)
        held = jnp.stack(placed).reshape((2,) * len(group) + held.shape)
        axis_bits = group[::-1] + axis_bits
    order = sorted(range(len(axis_bits)), key=lambda k: -axis_bits[k])
    held = jnp.transpose(held, order + list(range(len(axis_bits), held.ndim)))
    return held.reshape((size,) + block.shape)


def scattered_sum(rows, axis, groups):
    size = lax.axis_size(axis)
    index = lax.axis_index(axis)
    held = rows.reshape((size, rows.shape[0] // size) + rows.shape[1:])
    low = 0
    for width in groups:
        ways = 1 << width
        held = held.reshape((held.shape[0] // ways, ways) + held.shape[1:])
        mine = index >> low & ways - 1
        total = lax.dynamic_index_in_dim(held, mine, axis=1, keepdims=False)
        for mask in range(1, ways):
            send = lax.dynamic_index_in_dim(held, mine ^ mask, axis=1, keepdims=False)
            flip = mask << low
            total = total + lax.ppermute(send, axis, [(i, i ^ flip) for i in range(size)])
        held = total
        low += width
    return held[0]


def slot_norm(raw_rows):
    parts = raw_rows.reshape(raw_rows.shape[0], 2 * KVH, HD)
    multiplier = lax.rsqrt(jnp.mean(parts * parts, axis=-1, keepdims=True) + norm_eps)
    return (parts * multiplier).reshape(raw_rows.shape)


def softmax_step(row_top, row_total, scores, allowed):
    scores = jnp.where(allowed, scores, neg_fill)
    new_top = jnp.maximum(row_top, jnp.max(scores, axis=-1))
    weights = jnp.where(allowed, jnp.exp(scores - new_top[..., None]), 0.0)
    multiplier = jnp.exp(row_top - new_top)
    new_total = row_total * multiplier + jnp.sum(weights, axis=-1)
    return (new_top, new_total, weights.astype(jnp.bfloat16), multiplier)


def shards(
    seg_queries, seg_keys, seg_values, grad_out, mem_init, mem_query, retention, seg_len, doc_start
):
    tok_rows = seg_queries.shape[1]
    mem_rows = mem_query.shape[0]
    group_size = QH // KVH
    width_kv = KVH * HD
    seg_count = lax.axis_size("seg")
    seg_index = lax.axis_index("seg")
    tok_index = lax.axis_index("tok")
    length = seg_len[seg_index]
    score_scale = 1.0 / math.sqrt(HD)
    queries = seg_queries[0].reshape(tok_rows, KVH, group_size, HD)
    slot_queries = mem_query.reshape(mem_rows, KVH, HD)
    row_pos = tok_index * tok_rows + jnp.arange(tok_rows)
    kv_piece = lax.all_gather(
        jnp.concatenate([seg_keys[0], seg_values[0]], axis=1), "tok", axis=0, tiled=True
    )
    piece_rows = kv_piece.shape[0]
    key_piece = kv_piece[:, :width_kv].reshape(piece_rows, KVH, HD)
    value_piece = kv_piece[:, width_kv:].reshape(piece_rows, KVH, HD)
    live_keys = jnp.arange(piece_rows) < length
    slot_scores = (
        jnp.einsum("rgd,ugd->gru", slot_queries, key_piece, preferred_element_type=jnp.float32)
        * score_scale
    )
    slot_scores = jnp.where(live_keys, slot_scores, neg_fill)
    slot_top = jnp.max(slot_scores, axis=-1, keepdims=True)
    slot_exp = jnp.where(live_keys, jnp.exp(slot_scores - slot_top), 0.0)
    slot_denom = jnp.transpose(jnp.sum(slot_exp, axis=-1))[..., None]
    slot_weights = slot_exp.astype(jnp.bfloat16)
    slot_keys = jnp.einsum(
        "gru,ugd->rgd", slot_weights, key_piece, preferred_element_type=jnp.float32
    )
    slot_values = jnp.einsum(
        "gru,ugd->rgd", slot_weights, value_piece, preferred_element_type=jnp.float32
    )
    raw_slots = jnp.concatenate(
        [
            (slot_keys / slot_denom).reshape(mem_rows, width_kv),
            (slot_values / slot_denom).reshape(mem_rows, width_kv),
        ],
        axis=1,
    )
    written = slot_norm(raw_slots)
    ret_row = retention[0]
    following = doc_start[jnp.minimum(seg_index + 1, seg_count - 1)].astype(jnp.float32)
    keep_flag = jnp.where(seg_index == seg_count - 1, 1.0, 1.0 - following)
    decay_rate = keep_flag * ret_row
    carried = keep_flag * (1.0 - ret_row) * written + (1.0 - keep_flag) * mem_init
    chain_terms = gathered(
        jnp.concatenate([carried, decay_rate[None]], axis=0), "seg", ((2, 3), (0, 1))
    )
    all_carried = chain_terms[:, :mem_rows]
    all_decay = chain_terms[:, mem_rows]
    memory_in = mem_init
    for step in range(seg_count - 1):
        following_memory = all_decay[step] * memory_in + all_carried[step]
        memory_in = jnp.where(step < seg_index, following_memory, memory_in)
    block_rows = math.gcd(piece_rows, 1024)
    blocks = piece_rows // block_rows
    running = (
        jnp.full((KVH, group_size, tok_rows), neg_fill, jnp.float32),
        jnp.zeros((KVH, group_size, tok_rows), jnp.float32),
        jnp.zeros((tok_rows, KVH, group_size, HD), jnp.float32),
    )
    for block in range(blocks):
        block_start = block * block_rows
        key_block = key_piece[block_start : block_start + block_rows]
        value_block = value_piece[block_start : block_start + block_rows]
        columns = block_start + jnp.arange(block_rows)
        causal = (columns[None, :] <= row_pos[:, None]) & (columns < length)[None, :]
        seg_scores = (
            jnp.einsum("tgjd,ugd->gjtu", queries, key_block, preferred_element_type=jnp.float32)
            * score_scale
        )
        seg_top, seg_total, seg_weights, seg_factor = softmax_step(
            running[0], running[1], seg_scores, causal
        )
        seg_acc = running[2] * jnp.transpose(seg_factor, (2, 0, 1))[..., None] + jnp.einsum(
            "gjtu,ugd->tgjd", seg_weights, value_block, preferred_element_type=jnp.float32
        )
        running = (seg_top, seg_total, seg_acc)
    memory_all = gathered(memory_in.astype(jnp.bfloat16), "tok", ((3, 4), (1, 2), (0,))).reshape(
        -1, 2 * width_kv
    )
    mem_keys = memory_all[:, :width_kv].reshape(-1, KVH, HD)
    mem_vals = memory_all[:, width_kv:].reshape(-1, KVH, HD)
    mem_scores = (
        jnp.einsum("tgjd,mgd->gjtm", queries, mem_keys, preferred_element_type=jnp.float32)
        * score_scale
    )
    row_top = jnp.maximum(running[0], jnp.max(mem_scores, axis=-1))
    seg_factor = jnp.exp(running[0] - row_top)
    mem_weights = jnp.exp(mem_scores - row_top[..., None])
    row_total = running[1] * seg_factor + jnp.sum(mem_weights, axis=-1)
    weighted = running[2] * jnp.transpose(seg_factor, (2, 0, 1))[..., None] + jnp.einsum(
        "gjtm,mgd->tgjd",
        mem_weights.astype(jnp.bfloat16),
        mem_vals,
        preferred_element_type=jnp.float32,
    )
    att_rows = weighted / jnp.transpose(row_total, (2, 0, 1))[..., None]
    log_total = row_top + jnp.log(row_total)
    attended = att_rows.reshape(1, tok_rows, QH * HD).astype(jnp.bfloat16)
    valid_rows = (row_pos < length).astype(jnp.bfloat16)[:, None]
    cotangent = (grad_out[0] * valid_rows * loss_scale).reshape(tok_rows, KVH, group_size, HD)
    row_delta = jnp.einsum("tgjd,tgjd->gjt", cotangent.astype(jnp.float32), att_rows)
    mem_prob = jnp.exp(mem_scores - log_total[..., None])
    grad_prob = jnp.einsum(
        "tgjd,mgd->gjtm", cotangent, mem_vals, preferred_element_type=jnp.float32
    )
    grad_score = mem_prob * (grad_prob - row_delta[..., None])
    grad_vals = jnp.einsum(
        "gjtm,tgjd->mgd",
        mem_prob.astype(jnp.bfloat16),
        cotangent,
        preferred_element_type=jnp.float32,
    )
    grad_keys = (
        jnp.einsum(
            "gjtm,tgjd->mgd",
            grad_score.astype(jnp.bfloat16),
            queries,
            preferred_element_type=jnp.float32,
        )
        * score_scale
    )
    grad_slots = jnp.concatenate(
        [grad_keys.reshape(-1, width_kv), grad_vals.reshape(-1, width_kv)], axis=1
    )
    local_grad = scattered_sum(grad_slots, "tok", (1, 2, 2))
    all_local = gathered(local_grad, "seg", ((2, 3), (0, 1)))
    memory_grad = all_local[seg_count - 1]
    for step in range(seg_count - 2, -1, -1):
        earlier_grad = all_local[step] + all_decay[step] * memory_grad
        memory_grad = jnp.where(step >= seg_index, earlier_grad, memory_grad)
    return (attended, memory_in[None], memory_grad[None])


def solution(mesh):
    placed = (
        P("seg", "tok", None),
        P("seg", "tok", None),
        P("seg", "tok", None),
        P("seg", "tok", None),
        P("tok", None),
        P("tok", None),
        P("seg", None),
        P(),
        P(),
    )
    return jax.shard_map(
        shards,
        mesh=mesh,
        in_specs=placed,
        out_specs=(P("seg", "tok", None), P("seg", "tok", None), P("seg", "tok", None)),
        check_vma=False,
    )
```

profile of v0, /device:TPU:2, one launch (start us, length us, event | category | flops | bytes accessed | tf_op | source)
XLA Modules:
  0.0 347.7 jit_solution(11766808417356156304)
XLA Ops:
  22.1 106.7 %all-gather.2.cloned.1.call-done = bf16[4096,1024]{0,1:T(8,128)(2,1)} async-done(((bf16[128,1024]{0,1:T(8,128)(2,1)}), bf16[4096,1024]{0,1:T(8,128)(2,1)}) %all-gather.2.cloned.1.call-update) | async-done | bytes 8388624 | tf_op jit(solution)/shard_map/all_gather | solution.py:89
  128.8 6.1 %fusion.185 = (bf16[4096,512]{0,1:T(8,128)(2,1)}, bf16[4096,512]{0,1:T(8,128)(2,1)}) fusion(bf16[4096,1024]{0,1:T(8,128)(2,1)} %all-gather.2.cloned.1.call-done), kind=kLoop, calls=%fused_computation.282 | loop fusion | bytes 16777216 | tf_op jit(solution)/shard_map/slice | solution.py:93
  134.9 3.1 fusion.188
  138.0 3.5 %fusion.80 = f32[8,4,128]{2,0,1:T(8,128)S(1)} fusion(bf16[4096,4,128]{0,2,1:T(8,128)(2,1)} %bitcast.616, bf16[4,8,4096]{2,1,0:T(8,128)(2,1)S(1)} %get-tuple-element.90, f32[8,4]{0,1:T(4,128)S(1)} %bitcast.687), kind=kOutput, calls=%fused_computation.70 | convolution fusion | flops 33558528 | bytes 4472960 | tf_op jit(solution)/shard_map/gru,ugd->rgd/dot_general | solution.py:105
  141.6 3.5 %fusion.79 = f32[8,4,128]{2,0,1:T(8,128)S(1)} fusion(bf16[4096,4,128]{0,2,1:T(8,128)(2,1)} %bitcast.614, bf16[4,8,4096]{2,1,0:T(8,128)(2,1)S(1)} %get-tuple-element.90, f32[8,4]{0,1:T(4,128)S(1)} %bitcast.688), kind=kOutput, calls=%fused_computation.68 | convolution fusion | flops 33558528 | bytes 4472960 | tf_op jit(solution)/shard_map/gru,ugd->rgd/dot_general | solution.py:108
  145.3 6.6 %collective-permute-start = (f32[1,9,1024]{2,1,0:T(8,128)S(1)}, f32[1,9,1024]{2,1,0:T(8,128)S(1)}, u32[]{:S(2)}, u32[]{:S(2)}) collective-permute-start(f32[1,9,1024]{2,1,0:T(8,128)S(1)} %maximum_bitcast_fusion.1), channel_id=1, source_target_pairs={{0,384},{32,416},{64,448},{96,480},{128,256},{160,288},{192,320},{... | collective-permute-start | bytes 110600 | tf_op jit(solution)/shard_map/ppermute | solution.py:26
  151.9 3.5 %collective-permute-start.1 = (f32[1,9,1024]{2,1,0:T(8,128)S(1)}, f32[1,9,1024]{2,1,0:T(8,128)S(1)}, u32[]{:S(2)}, u32[]{:S(2)}) collective-permute-start(f32[1,9,1024]{2,1,0:T(8,128)S(1)} %maximum_bitcast_fusion.1), channel_id=1, source_target_pairs={{0,256},{32,288},{64,320},{96,352},{128,384},{160,416},{192,448},{... | collective-permute-start | bytes 110600 | tf_op jit(solution)/shard_map/ppermute | solution.py:26
  167.0 4.4 %collective-permute-start.4 = (f32[2,2,1,9,1024]{4,3,1,0,2:T(8,128)S(1)}, f32[2,2,1,9,1024]{4,3,1,0,2:T(8,128)S(1)}, u32[]{:S(2)}, u32[]{:S(2)}) collective-permute-start(f32[2,2,1,9,1024]{4,3,1,0,2:T(8,128)S(1)} %bitcast.636), channel_id=1, source_target_pairs={{0,64},{32,96},{64,0},{96,32},{128,192},{160,224},{192,128},{224,1... | collective-permute-start | bytes 442376 | tf_op jit(solution)/shard_map/ppermute | solution.py:26
  174.0 4.9 %fusion.4 = (f32[4,4,128]{2,1,0:T(4,128)S(1)}, f32[4,1024,128,4]{2,1,3,0:T(8,128)}) fusion(pred[128,1024]{0,1:T(8,128)(4,1)S(1)} %get-tuple-element.86, bf16[1024,4,128,1]{0,2,3,1:T(8,128)(2,1)S(1)} %bitcast.620, bf16[128,4,4,128]{3,2,1,0:T(4,128)(2,1)S(1)} %reshape_squeeze.3), kind=kOutput, calls=%fused_computation.12 | convolution fusion | flops 543160320 | bytes 10100736 | tf_op jit(solution)/shard_map/tgjd,ugd->gjtu/dot_general | solution.py:147
  182.9 4.9 %collective-permute-start.6 = (bf16[1,8,1024]{2,1,0:T(8,128)(2,1)S(1)}, bf16[1,8,1024]{2,1,0:T(8,128)(2,1)S(1)}, u32[]{:S(2)}, u32[]{:S(2)}) collective-permute-start(bf16[1,8,1024]{2,1,0:T(8,128)(2,1)S(1)} %get-tuple-element.20), channel_id=1, source_target_pairs={{0,24},{1,25},{2,26},{3,27},{4,28},{5,29},{6,30},{7,31},{8,16},{9,... | collective-permute-start | bytes 49160 | tf_op jit(solution)/shard_map/ppermute | solution.py:26
  187.9 4.4 %collective-permute-start.7 = (bf16[1,8,1024]{2,1,0:T(8,128)(2,1)S(1)}, bf16[1,8,1024]{2,1,0:T(8,128)(2,1)S(1)}, u32[]{:S(2)}, u32[]{:S(2)}) collective-permute-start(bf16[1,8,1024]{2,1,0:T(8,128)(2,1)S(1)} %get-tuple-element.20), channel_id=1, source_target_pairs={{0,16},{1,17},{2,18},{3,19},{4,20},{5,21},{6,22},{7,23},{8,24},{9,... | collective-permute-start | bytes 49160 | tf_op jit(solution)/shard_map/ppermute | solution.py:26
  192.3 5.3 %collective-permute-start.8 = (bf16[1,8,1024]{2,1,0:T(8,128)(2,1)S(1)}, bf16[1,8,1024]{2,1,0:T(8,128)(2,1)S(1)}, u32[]{:S(2)}, u32[]{:S(2)}) collective-permute-start(bf16[1,8,1024]{2,1,0:T(8,128)(2,1)S(1)} %get-tuple-element.20), channel_id=1, source_target_pairs={{0,8},{1,9},{2,10},{3,11},{4,12},{5,13},{6,14},{7,15},{8,0},{9,1},... | collective-permute-start | bytes 49160 | tf_op jit(solution)/shard_map/ppermute | solution.py:26
  197.7 5.5 %fusion.3 = (f32[4,4,128]{2,1,0:T(4,128)}, f32[4,1024,128,4]{2,1,3,0:T(8,128)}) fusion(pred[128,1024]{0,1:T(8,128)(4,1)S(1)} %get-tuple-element.85, bf16[1024,4,128,1]{0,2,3,1:T(8,128)(2,1)S(1)} %bitcast.619, bf16[128,4,4,128]{3,2,1,0:T(4,128)(2,1)S(1)} %reshape_squeeze.3), kind=kOutput, calls=%fused_computation.11 | convolution fusion | flops 543160320 | bytes 10100736 | tf_op jit(solution)/shard_map/tgjd,ugd->gjtu/dot_general | solution.py:147
  203.2 4.0 %collective-permute-start.9 = (bf16[2,2,1,8,1024]{4,3,1,0,2:T(8,128)(2,1)S(1)}, bf16[2,2,1,8,1024]{4,3,1,0,2:T(8,128)(2,1)S(1)}, u32[]{:S(2)}, u32[]{:S(2)}) collective-permute-start(bf16[2,2,1,8,1024]{4,3,1,0,2:T(8,128)(2,1)S(1)} %bitcast.651), channel_id=1, source_target_pairs={{0,6},{1,7},{2,4},{3,5},{4,2},{5,3},{6,0},{7,1},{8,14},{9,15},{10,... | collective-permute-start | bytes 196616 | tf_op jit(solution)/shard_map/ppermute | solution.py:26
  210.0 3.3 collective-permute-start.11
  213.3 5.5 %fusion.2 = (f32[4,4,128]{2,1,0:T(4,128)}, f32[4,1024,128,4]{2,1,3,0:T(8,128)}) fusion(pred[128,1024]{0,1:T(8,128)(4,1)S(1)} %get-tuple-element.87, bf16[1024,4,128,1]{0,2,3,1:T(8,128)(2,1)S(1)} %bitcast.618, bf16[128,4,4,128]{3,2,1,0:T(4,128)(2,1)S(1)} %reshape_squeeze.3), kind=kOutput, calls=%fused_computation.10 | convolution fusion | flops 543160320 | bytes 10100736 | tf_op jit(solution)/shard_map/tgjd,ugd->gjtu/dot_general | solution.py:147
  221.1 4.8 %fusion.1 = (f32[4,4,128]{2,1,0:T(4,128)S(1)}, f32[4,1024,128,4]{2,1,3,0:T(8,128)}) fusion(pred[128,1024]{0,1:T(8,128)(4,1)S(1)} %copy-done.3, bf16[1024,4,128,1]{0,2,3,1:T(8,128)(2,1)S(1)} %bitcast.617, bf16[128,4,4,128]{3,2,1,0:T(4,128)(2,1)S(1)} %reshape_squeeze.3), kind=kOutput, calls=%fused_computation.9 | convolution fusion | flops 543160320 | bytes 10100736 | tf_op jit(solution)/shard_map/tgjd,ugd->gjtu/dot_general | solution.py:147
  230.2 4.6 %fusion.11 = f32[4,4,128]{2,1,0:T(4,128)S(1)} fusion(f32[4,1024,128,4]{2,1,3,0:T(8,128)} %get-tuple-element.94, f32[4,4,128]{2,1,0:T(4,128)S(1)} %get-tuple-element.17, pred[128,1024]{0,1:T(8,128)(4,1)S(1)} %get-tuple-element.86), kind=kLoop, calls=%fused_computation.19 | loop fusion | flops 10483712 | bytes 8536064 | tf_op jit(solution)/shard_map/reduce_sum | solution.py:70
  234.8 4.8 %fusion.9 = f32[4,4,128]{2,1,0:T(4,128)S(1)} fusion(f32[4,1024,128,4]{2,1,3,0:T(8,128)} %get-tuple-element.96, f32[4,4,128]{2,1,0:T(4,128)S(1)} %get-tuple-element.18, pred[128,1024]{0,1:T(8,128)(4,1)S(1)} %get-tuple-element.85), kind=kLoop, calls=%fused_computation.17 | loop fusion | flops 10483712 | bytes 8536064 | tf_op jit(solution)/shard_map/reduce_sum | solution.py:70
  246.5 5.9 %fusion.64 = f32[128,4,4,128]{0,3,2,1:T(8,128)S(1)} fusion(bf16[1024,4,128,1]{0,2,3,1:T(8,128)(2,1)} %bitcast.634, f32[4,1024,128,4]{2,1,3,0:T(8,128)} %get-tuple-element.100, f32[4,4,128]{2,1,0:T(4,128)} %copy-done.52, pred[128,1024]{0,1:T(8,128)(4,1)} %get-tuple-element.88, f32[128,4,4]{0,2,1:T(4,128)} %get-tuple-element.80, ...), kind=kOutput, calls=%fused_computation.59 | convolution fusion | flops 547880960 | bytes 10641408 | tf_op jit(solution)/shard_map/gjtu,ugd->tgjd/dot_general | solution.py:153
  252.5 5.7 %fusion.67 = f32[128,4,4,128]{0,3,2,1:T(8,128)S(1)} fusion(f32[128,4,4,128]{0,3,2,1:T(8,128)S(1)} %fusion.64, bf16[1024,4,128,1]{0,2,3,1:T(8,128)(2,1)S(1)} %bitcast.633, f32[4,1024,128,4]{2,1,3,0:T(8,128)} %get-tuple-element.98, f32[4,4,128]{2,1,0:T(4,128)S(1)} %copy-done.21, pred[128,1024]{0,1:T(8,128)(4,1)S(1)} %get-tuple-element.87, ...), kind=kOutput, calls=%fused_computation.60 | convolution fusion | flops 547880960 | bytes 11681792 | tf_op jit(solution)/shard_map/gjtu,ugd->tgjd/dot_general | solution.py:153
  275.6 4.0 %collective-permute-start.16 = (f32[4,8,1024]{2,1,0:T(8,128)S(1)}, f32[4,8,1024]{2,1,0:T(8,128)S(1)}, u32[]{:S(2)}, u32[]{:S(2)}) collective-permute-start(f32[4,8,1024]{2,1,0:T(8,128)S(1)} %get-tuple-element.56), channel_id=1, source_target_pairs={{0,6},{1,7},{2,4},{3,5},{4,2},{5,3},{6,0},{7,1},{8,14},{9,15},{10,... | collective-permute-start | bytes 393224 | tf_op jit(solution)/shard_map/ppermute | solution.py:53
  281.6 4.1 %collective-permute-start.14 = (f32[4,8,1024]{2,1,0:T(8,128)S(1)}, f32[4,8,1024]{2,1,0:T(8,128)S(1)}, u32[]{:S(2)}, u32[]{:S(2)}) collective-permute-start(f32[4,8,1024]{2,1,0:T(8,128)S(1)} %get-tuple-element.55), channel_id=1, source_target_pairs={{0,2},{1,3},{2,0},{3,1},{4,6},{5,7},{6,4},{7,5},{8,10},{9,11},{10,... | collective-permute-start | bytes 393224 | tf_op jit(solution)/shard_map/ppermute | solution.py:53
  285.8 6.1 %collective-permute-done.15 = f32[4,8,1024]{2,1,0:T(8,128)S(1)} collective-permute-done((f32[4,8,1024]{2,1,0:T(8,128)S(1)}, f32[4,8,1024]{2,1,0:T(8,128)S(1)}, u32[]{:S(2)}, u32[]{:S(2)}) %collective-permute-start.15) | collective-permute-done | bytes 131104 | tf_op jit(solution)/shard_map/ppermute | solution.py:53
  292.1 5.8 %collective-permute-start.19 = (f32[1,8,1024]{2,1,0:T(8,128)S(1)}, f32[1,8,1024]{2,1,0:T(8,128)S(1)}, u32[]{:S(2)}, u32[]{:S(2)}) collective-permute-start(f32[1,8,1024]{2,1,0:T(8,128)S(1)} %get-tuple-element.74), channel_id=1, source_target_pairs={{0,24},{1,25},{2,26},{3,27},{4,28},{5,29},{6,30},{7,31},{8,16},{9,... | collective-permute-start | bytes 98312 | tf_op jit(solution)/shard_map/ppermute | solution.py:53
  297.9 4.4 %collective-permute-start.18 = (f32[1,8,1024]{2,1,0:T(8,128)S(1)}, f32[1,8,1024]{2,1,0:T(8,128)S(1)}, u32[]{:S(2)}, u32[]{:S(2)}) collective-permute-start(f32[1,8,1024]{2,1,0:T(8,128)S(1)} %get-tuple-element.75), channel_id=1, source_target_pairs={{0,16},{1,17},{2,18},{3,19},{4,20},{5,21},{6,22},{7,23},{8,24},{9,... | collective-permute-start | bytes 98312 | tf_op jit(solution)/shard_map/ppermute | solution.py:53
  302.3 4.4 %collective-permute-start.17 = (f32[1,8,1024]{2,1,0:T(8,128)S(1)}, f32[1,8,1024]{2,1,0:T(8,128)S(1)}, u32[]{:S(2)}, u32[]{:S(2)}) collective-permute-start(f32[1,8,1024]{2,1,0:T(8,128)S(1)} %get-tuple-element.73), channel_id=1, source_target_pairs={{0,8},{1,9},{2,10},{3,11},{4,12},{5,13},{6,14},{7,15},{8,0},{9,1},... | collective-permute-start | bytes 98312 | tf_op jit(solution)/shard_map/ppermute | solution.py:53
  306.8 5.4 %collective-permute-done.17 = f32[1,8,1024]{2,1,0:T(8,128)S(1)} collective-permute-done((f32[1,8,1024]{2,1,0:T(8,128)S(1)}, f32[1,8,1024]{2,1,0:T(8,128)S(1)}, u32[]{:S(2)}, u32[]{:S(2)}) %collective-permute-start.17) | collective-permute-done | bytes 32800 | tf_op jit(solution)/shard_map/ppermute | solution.py:53
  312.2 3.3 collective-permute-start.20
  315.6 4.3 %collective-permute-start.21 = (f32[1,8,1024]{2,1,0:T(8,128)S(1)}, f32[1,8,1024]{2,1,0:T(8,128)S(1)}, u32[]{:S(2)}, u32[]{:S(2)}) collective-permute-start(f32[1,8,1024]{2,1,0:T(8,128)S(1)} %add_add_fusion), channel_id=1, source_target_pairs={{0,256},{32,288},{64,320},{96,352},{128,384},{160,416},{192,448},{... | collective-permute-start | bytes 98312 | tf_op jit(solution)/shard_map/ppermute | solution.py:26
  319.9 4.6 %collective-permute-start.22 = (f32[1,8,1024]{2,1,0:T(8,128)S(1)}, f32[1,8,1024]{2,1,0:T(8,128)S(1)}, u32[]{:S(2)}, u32[]{:S(2)}) collective-permute-start(f32[1,8,1024]{2,1,0:T(8,128)S(1)} %add_add_fusion), channel_id=1, source_target_pairs={{0,128},{32,160},{64,192},{96,224},{128,0},{160,32},{192,64},{224,... | collective-permute-start | bytes 98312 | tf_op jit(solution)/shard_map/ppermute | solution.py:26
  326.7 3.9 %collective-permute-start.23 = (f32[2,2,1,8,1024]{4,3,1,0,2:T(8,128)S(1)}, f32[2,2,1,8,1024]{4,3,1,0,2:T(8,128)S(1)}, u32[]{:S(2)}, u32[]{:S(2)}) collective-permute-start(f32[2,2,1,8,1024]{4,3,1,0,2:T(8,128)S(1)} %bitcast.645), channel_id=1, source_target_pairs={{0,96},{32,64},{64,32},{96,0},{128,224},{160,192},{192,160},{224,1... | collective-permute-start | bytes 393224 | tf_op jit(solution)/shard_map/ppermute | solution.py:26
  (244 shorter events, 79.8 us)
Async XLA Ops:
  7.2 127.8 %copy-start = (bf16[8,512]{1,0:T(8,128)(2,1)S(1)}, bf16[8,512]{1,0:T(8,128)(2,1)}, u32[]{:S(2)}) copy-start(bf16[8,512]{1,0:T(8,128)(2,1)} %param.14) | copy-start | bytes 24580
  7.2 121.6 %all-gather.2.cloned.1.call-start = ((), (), s32[]{:S(2)}) async-start(), calls=%async_computation | async-start | bytes 8650752 | tf_op jit(solution)/shard_map/all_gather | solution.py:89
  145.3 15.2 %collective-permute-start = (f32[1,9,1024]{2,1,0:T(8,128)S(1)}, f32[1,9,1024]{2,1,0:T(8,128)S(1)}, u32[]{:S(2)}, u32[]{:S(2)}) collective-permute-start(f32[1,9,1024]{2,1,0:T(8,128)S(1)} %maximum_bitcast_fusion.1), channel_id=1, source_target_pairs={{0,384},{32,416},{64,448},{96,480},{128,256},{160,288},{192,320},{... | collective-permute-start | bytes 110600 | tf_op jit(solution)/shard_map/ppermute | solution.py:26
  151.9 11.0 %collective-permute-start.1 = (f32[1,9,1024]{2,1,0:T(8,128)S(1)}, f32[1,9,1024]{2,1,0:T(8,128)S(1)}, u32[]{:S(2)}, u32[]{:S(2)}) collective-permute-start(f32[1,9,1024]{2,1,0:T(8,128)S(1)} %maximum_bitcast_fusion.1), channel_id=1, source_target_pairs={{0,256},{32,288},{64,320},{96,352},{128,384},{160,416},{192,448},{... | collective-permute-start | bytes 110600 | tf_op jit(solution)/shard_map/ppermute | solution.py:26
  155.4 9.2 %collective-permute-start.2 = (f32[1,9,1024]{2,1,0:T(8,128)S(1)}, f32[1,9,1024]{2,1,0:T(8,128)S(1)}, u32[]{:S(2)}, u32[]{:S(2)}) collective-permute-start(f32[1,9,1024]{2,1,0:T(8,128)S(1)} %maximum_bitcast_fusion.1), channel_id=1, source_target_pairs={{0,128},{32,160},{64,192},{96,224},{128,0},{160,32},{192,64},{224,... | collective-permute-start | bytes 110600 | tf_op jit(solution)/shard_map/ppermute | solution.py:26
  164.7 14.1 %collective-permute-start.3 = (f32[2,2,1,9,1024]{4,3,1,0,2:T(8,128)S(1)}, f32[2,2,1,9,1024]{4,3,1,0,2:T(8,128)S(1)}, u32[]{:S(2)}, u32[]{:S(2)}) collective-permute-start(f32[2,2,1,9,1024]{4,3,1,0,2:T(8,128)S(1)} %bitcast.635), channel_id=1, source_target_pairs={{0,96},{32,64},{64,32},{96,0},{128,224},{160,192},{192,160},{224,1... | collective-permute-start | bytes 442376 | tf_op jit(solution)/shard_map/ppermute | solution.py:26
  167.0 14.1 %collective-permute-start.4 = (f32[2,2,1,9,1024]{4,3,1,0,2:T(8,128)S(1)}, f32[2,2,1,9,1024]{4,3,1,0,2:T(8,128)S(1)}, u32[]{:S(2)}, u32[]{:S(2)}) collective-permute-start(f32[2,2,1,9,1024]{4,3,1,0,2:T(8,128)S(1)} %bitcast.636), channel_id=1, source_target_pairs={{0,64},{32,96},{64,0},{96,32},{128,192},{160,224},{192,128},{224,1... | collective-permute-start | bytes 442376 | tf_op jit(solution)/shard_map/ppermute | solution.py:26
  171.5 10.1 %collective-permute-start.5 = (f32[2,2,1,9,1024]{4,3,1,0,2:T(8,128)S(1)}, f32[2,2,1,9,1024]{4,3,1,0,2:T(8,128)S(1)}, u32[]{:S(2)}, u32[]{:S(2)}) collective-permute-start(f32[2,2,1,9,1024]{4,3,1,0,2:T(8,128)S(1)} %bitcast.637), channel_id=1, source_target_pairs={{0,32},{32,0},{64,96},{96,64},{128,160},{160,128},{192,224},{224,1... | collective-permute-start | bytes 442376 | tf_op jit(solution)/shard_map/ppermute | solution.py:26
  182.9 20.2 %collective-permute-start.6 = (bf16[1,8,1024]{2,1,0:T(8,128)(2,1)S(1)}, bf16[1,8,1024]{2,1,0:T(8,128)(2,1)S(1)}, u32[]{:S(2)}, u32[]{:S(2)}) collective-permute-start(bf16[1,8,1024]{2,1,0:T(8,128)(2,1)S(1)} %get-tuple-element.20), channel_id=1, source_target_pairs={{0,24},{1,25},{2,26},{3,27},{4,28},{5,29},{6,30},{7,31},{8,16},{9,... | collective-permute-start | bytes 49160 | tf_op jit(solution)/shard_map/ppermute | solution.py:26
  187.9 15.3 %collective-permute-start.7 = (bf16[1,8,1024]{2,1,0:T(8,128)(2,1)S(1)}, bf16[1,8,1024]{2,1,0:T(8,128)(2,1)S(1)}, u32[]{:S(2)}, u32[]{:S(2)}) collective-permute-start(bf16[1,8,1024]{2,1,0:T(8,128)(2,1)S(1)} %get-tuple-element.20), channel_id=1, source_target_pairs={{0,16},{1,17},{2,18},{3,19},{4,20},{5,21},{6,22},{7,23},{8,24},{9,... | collective-permute-start | bytes 49160 | tf_op jit(solution)/shard_map/ppermute | solution.py:26
  192.3 10.9 %collective-permute-start.8 = (bf16[1,8,1024]{2,1,0:T(8,128)(2,1)S(1)}, bf16[1,8,1024]{2,1,0:T(8,128)(2,1)S(1)}, u32[]{:S(2)}, u32[]{:S(2)}) collective-permute-start(bf16[1,8,1024]{2,1,0:T(8,128)(2,1)S(1)} %get-tuple-element.20), channel_id=1, source_target_pairs={{0,8},{1,9},{2,10},{3,11},{4,12},{5,13},{6,14},{7,15},{8,0},{9,1},... | collective-permute-start | bytes 49160 | tf_op jit(solution)/shard_map/ppermute | solution.py:26
  203.2 15.6 %collective-permute-start.9 = (bf16[2,2,1,8,1024]{4,3,1,0,2:T(8,128)(2,1)S(1)}, bf16[2,2,1,8,1024]{4,3,1,0,2:T(8,128)(2,1)S(1)}, u32[]{:S(2)}, u32[]{:S(2)}) collective-permute-start(bf16[2,2,1,8,1024]{4,3,1,0,2:T(8,128)(2,1)S(1)} %bitcast.651), channel_id=1, source_target_pairs={{0,6},{1,7},{2,4},{3,5},{4,2},{5,3},{6,0},{7,1},{8,14},{9,15},{10,... | collective-permute-start | bytes 196616 | tf_op jit(solution)/shard_map/ppermute | solution.py:26
  207.3 11.6 %collective-permute-start.10 = (bf16[2,2,1,8,1024]{4,3,1,0,2:T(8,128)(2,1)S(1)}, bf16[2,2,1,8,1024]{4,3,1,0,2:T(8,128)(2,1)S(1)}, u32[]{:S(2)}, u32[]{:S(2)}) collective-permute-start(bf16[2,2,1,8,1024]{4,3,1,0,2:T(8,128)(2,1)S(1)} %bitcast.652), channel_id=1, source_target_pairs={{0,4},{1,5},{2,6},{3,7},{4,0},{5,1},{6,2},{7,3},{8,12},{9,13},{10,... | collective-permute-start | bytes 196616 | tf_op jit(solution)/shard_map/ppermute | solution.py:26
  210.0 8.9 %collective-permute-start.11 = (bf16[2,2,1,8,1024]{4,3,1,0,2:T(8,128)(2,1)S(1)}, bf16[2,2,1,8,1024]{4,3,1,0,2:T(8,128)(2,1)S(1)}, u32[]{:S(2)}, u32[]{:S(2)}) collective-permute-start(bf16[2,2,1,8,1024]{4,3,1,0,2:T(8,128)(2,1)S(1)} %bitcast.653), channel_id=1, source_target_pairs={{0,2},{1,3},{2,0},{3,1},{4,6},{5,7},{6,4},{7,5},{8,10},{9,11},{10,... | collective-permute-start | bytes 196616 | tf_op jit(solution)/shard_map/ppermute | solution.py:26
  218.9 6.9 %collective-permute-start.12 = (bf16[2,2,2,2,1,8,1024]{6,5,3,2,1,0,4:T(8,128)(2,1)S(1)}, bf16[2,2,2,2,1,8,1024]{6,5,3,2,1,0,4:T(8,128)(2,1)S(1)}, u32[]{:S(2)}, u32[]{:S(2)}) collective-permute-start(bf16[2,2,2,2,1,8,1024]{6,5,3,2,1,0,4:T(8,128)(2,1)S(1)} %bitcast.639), channel_id=1, source_target_pairs={{0,1},{1,0},{2,3},{3,2},{4,5},{5,4},{6,7},{7,6},{8,9},{9,8},{10,11... | collective-permute-start | bytes 786440 | tf_op jit(solution)/shard_map/ppermute | solution.py:26
  266.3 74.5 %copy-start.1 = (bf16[8,512]{1,0:T(8,128)(2,1)S(1)}, bf16[8,512]{1,0:T(8,128)(2,1)}, u32[]{:S(2)}) copy-start(bf16[8,512]{1,0:T(8,128)(2,1)} %param.14) | copy-start | bytes 24580
  268.1 71.9 %copy-start.29 = (f32[1,1,1024]{2,1,0:T(1,128)S(1)}, f32[1,1,1024]{2,1,0:T(1,128)}, u32[]{:S(2)}) copy-start(f32[1,1,1024]{2,1,0:T(1,128)} %copy-done.28) | copy-start | bytes 12292
  268.1 71.9 %copy-start.31 = (f32[1,1,1024]{2,1,0:T(1,128)S(1)}, f32[1,1,1024]{2,1,0:T(1,128)}, u32[]{:S(2)}) copy-start(f32[1,1,1024]{2,1,0:T(1,128)} %copy-done.30) | copy-start | bytes 12292
  268.2 71.9 %copy-start.33 = (f32[1,1,1024]{2,1,0:T(1,128)S(1)}, f32[1,1,1024]{2,1,0:T(1,128)}, u32[]{:S(2)}) copy-start(f32[1,1,1024]{2,1,0:T(1,128)} %copy-done.32) | copy-start | bytes 12292
  271.6 3.9 %collective-permute-start.13 = (f32[16,8,1024]{2,1,0:T(8,128)S(1)}, f32[16,8,1024]{2,1,0:T(8,128)S(1)}, u32[]{:S(2)}, u32[]{:S(2)}) collective-permute-start(f32[16,8,1024]{2,1,0:T(8,128)S(1)} %dynamic-slice_bitcast_fusion), channel_id=1, source_target_pairs={{0,1},{1,0},{2,3},{3,2},{4,5},{5,4},{6,7},{7,6},{8,9},{9,8},{10,11... | collective-permute-start | bytes 1572872 | tf_op jit(solution)/shard_map/ppermute | solution.py:53
  275.6 10.2 %collective-permute-start.16 = (f32[4,8,1024]{2,1,0:T(8,128)S(1)}, f32[4,8,1024]{2,1,0:T(8,128)S(1)}, u32[]{:S(2)}, u32[]{:S(2)}) collective-permute-start(f32[4,8,1024]{2,1,0:T(8,128)S(1)} %get-tuple-element.56), channel_id=1, source_target_pairs={{0,6},{1,7},{2,4},{3,5},{4,2},{5,3},{6,0},{7,1},{8,14},{9,15},{10,... | collective-permute-start | bytes 393224 | tf_op jit(solution)/shard_map/ppermute | solution.py:53
  279.7 12.2 %collective-permute-start.15 = (f32[4,8,1024]{2,1,0:T(8,128)S(1)}, f32[4,8,1024]{2,1,0:T(8,128)S(1)}, u32[]{:S(2)}, u32[]{:S(2)}) collective-permute-start(f32[4,8,1024]{2,1,0:T(8,128)S(1)} %get-tuple-element.57), channel_id=1, source_target_pairs={{0,4},{1,5},{2,6},{3,7},{4,0},{5,1},{6,2},{7,3},{8,12},{9,13},{10,... | collective-permute-start | bytes 393224 | tf_op jit(solution)/shard_map/ppermute | solution.py:53
  281.6 10.4 %collective-permute-start.14 = (f32[4,8,1024]{2,1,0:T(8,128)S(1)}, f32[4,8,1024]{2,1,0:T(8,128)S(1)}, u32[]{:S(2)}, u32[]{:S(2)}) collective-permute-start(f32[4,8,1024]{2,1,0:T(8,128)S(1)} %get-tuple-element.55), channel_id=1, source_target_pairs={{0,2},{1,3},{2,0},{3,1},{4,6},{5,7},{6,4},{7,5},{8,10},{9,11},{10,... | collective-permute-start | bytes 393224 | tf_op jit(solution)/shard_map/ppermute | solution.py:53
  292.1 14.7 %collective-permute-start.19 = (f32[1,8,1024]{2,1,0:T(8,128)S(1)}, f32[1,8,1024]{2,1,0:T(8,128)S(1)}, u32[]{:S(2)}, u32[]{:S(2)}) collective-permute-start(f32[1,8,1024]{2,1,0:T(8,128)S(1)} %get-tuple-element.74), channel_id=1, source_target_pairs={{0,24},{1,25},{2,26},{3,27},{4,28},{5,29},{6,30},{7,31},{8,16},{9,... | collective-permute-start | bytes 98312 | tf_op jit(solution)/shard_map/ppermute | solution.py:53
  297.9 8.8 %collective-permute-start.18 = (f32[1,8,1024]{2,1,0:T(8,128)S(1)}, f32[1,8,1024]{2,1,0:T(8,128)S(1)}, u32[]{:S(2)}, u32[]{:S(2)}) collective-permute-start(f32[1,8,1024]{2,1,0:T(8,128)S(1)} %get-tuple-element.75), channel_id=1, source_target_pairs={{0,16},{1,17},{2,18},{3,19},{4,20},{5,21},{6,22},{7,23},{8,24},{9,... | collective-permute-start | bytes 98312 | tf_op jit(solution)/shard_map/ppermute | solution.py:53
  302.3 9.9 %collective-permute-start.17 = (f32[1,8,1024]{2,1,0:T(8,128)S(1)}, f32[1,8,1024]{2,1,0:T(8,128)S(1)}, u32[]{:S(2)}, u32[]{:S(2)}) collective-permute-start(f32[1,8,1024]{2,1,0:T(8,128)S(1)} %get-tuple-element.73), channel_id=1, source_target_pairs={{0,8},{1,9},{2,10},{3,11},{4,12},{5,13},{6,14},{7,15},{8,0},{9,1},... | collective-permute-start | bytes 98312 | tf_op jit(solution)/shard_map/ppermute | solution.py:53
  312.2 12.2 %collective-permute-start.20 = (f32[1,8,1024]{2,1,0:T(8,128)S(1)}, f32[1,8,1024]{2,1,0:T(8,128)S(1)}, u32[]{:S(2)}, u32[]{:S(2)}) collective-permute-start(f32[1,8,1024]{2,1,0:T(8,128)S(1)} %add_add_fusion), channel_id=1, source_target_pairs={{0,384},{32,416},{64,448},{96,480},{128,256},{160,288},{192,320},{... | collective-permute-start | bytes 98312 | tf_op jit(solution)/shard_map/ppermute | solution.py:26
  315.6 10.0 %collective-permute-start.21 = (f32[1,8,1024]{2,1,0:T(8,128)S(1)}, f32[1,8,1024]{2,1,0:T(8,128)S(1)}, u32[]{:S(2)}, u32[]{:S(2)}) collective-permute-start(f32[1,8,1024]{2,1,0:T(8,128)S(1)} %add_add_fusion), channel_id=1, source_target_pairs={{0,256},{32,288},{64,320},{96,352},{128,384},{160,416},{192,448},{... | collective-permute-start | bytes 98312 | tf_op jit(solution)/shard_map/ppermute | solution.py:26
  319.9 6.7 %collective-permute-start.22 = (f32[1,8,1024]{2,1,0:T(8,128)S(1)}, f32[1,8,1024]{2,1,0:T(8,128)S(1)}, u32[]{:S(2)}, u32[]{:S(2)}) collective-permute-start(f32[1,8,1024]{2,1,0:T(8,128)S(1)} %add_add_fusion), channel_id=1, source_target_pairs={{0,128},{32,160},{64,192},{96,224},{128,0},{160,32},{192,64},{224,... | collective-permute-start | bytes 98312 | tf_op jit(solution)/shard_map/ppermute | solution.py:26
  326.7 10.3 %collective-permute-start.23 = (f32[2,2,1,8,1024]{4,3,1,0,2:T(8,128)S(1)}, f32[2,2,1,8,1024]{4,3,1,0,2:T(8,128)S(1)}, u32[]{:S(2)}, u32[]{:S(2)}) collective-permute-start(f32[2,2,1,8,1024]{4,3,1,0,2:T(8,128)S(1)} %bitcast.645), channel_id=1, source_target_pairs={{0,96},{32,64},{64,32},{96,0},{128,224},{160,192},{192,160},{224,1... | collective-permute-start | bytes 393224 | tf_op jit(solution)/shard_map/ppermute | solution.py:26
  330.5 6.9 %collective-permute-start.24 = (f32[2,2,1,8,1024]{4,3,1,0,2:T(8,128)S(1)}, f32[2,2,1,8,1024]{4,3,1,0,2:T(8,128)S(1)}, u32[]{:S(2)}, u32[]{:S(2)}) collective-permute-start(f32[2,2,1,8,1024]{4,3,1,0,2:T(8,128)S(1)} %bitcast.646), channel_id=1, source_target_pairs={{0,64},{32,96},{64,0},{96,32},{128,192},{160,224},{192,128},{224,1... | collective-permute-start | bytes 393224 | tf_op jit(solution)/shard_map/ppermute | solution.py:26
  332.9 6.9 %collective-permute-start.25 = (f32[2,2,1,8,1024]{4,3,1,0,2:T(8,128)S(1)}, f32[2,2,1,8,1024]{4,3,1,0,2:T(8,128)S(1)}, u32[]{:S(2)}, u32[]{:S(2)}) collective-permute-start(f32[2,2,1,8,1024]{4,3,1,0,2:T(8,128)S(1)} %bitcast.647), channel_id=1, source_target_pairs={{0,32},{32,0},{64,96},{96,64},{128,160},{160,128},{192,224},{224,1... | collective-permute-start | bytes 393224 | tf_op jit(solution)/shard_map/ppermute | solution.py:26
  (62 other events, 1467.9 us)
Sparse Core Ops, SparseCore 0:
  11.7 117.0 all-gather.1
where the time goes:
time: 349 us; the launch traced here: 348 us
  waiting for transfers between devices  132 us (38%)
  starting transfers between devices  97.4 us (28%)
  matrix products  53.2 us (15%)
  other arithmetic  24.5 us (7%)
  local copies, waits for them, and re-layouts  24.4 us (7%)
  between operations  16.4 us (5%)
    all_gather x1, waiting for transfers between devices, shards(): lax.all_gather(jnp.concatenate([seg_keys[0], seg_values[0]], axis=1), 'to...  107 us
    ppermute x19, starting transfers between devices, gathered(): lax.ppermute(held, axis, [(i, i ^ flip) for i in range(size)])  70.2 us
    ppermute x7, starting transfers between devices, scattered_sum(): lax.ppermute(send, axis, [(i, i ^ flip) for i in range(size)])  27.1 us
    dot_general x4, matrix products, shards(): jnp.einsum('tgjd,ugd->gjtu', queries, key_block, preferred_element_type=j...  20.6 us
    dot_general x4, matrix products, shards(): jnp.einsum('gjtu,ugd->tgjd', seg_weights, value_block, preferred_element_...  16.5 us
    reduce_sum x4, other arithmetic, softmax_step(): new_total = row_total * multiplier + jnp.sum(weights, axis=-1)  13.4 us
    ppermute x7, waiting for transfers between devices, scattered_sum(): lax.ppermute(send, axis, [(i, i ^ flip) for i in range(size)])  13.2 us
    ppermute x19, waiting for transfers between devices, gathered(): lax.ppermute(held, axis, [(i, i ^ flip) for i in range(size)])  11.8 us
  transfers between devices with their start and end apart: 27, of which 13 were waited for; matrix products, arithmetic and copies ran while one was open for 10% of the time, Pallas kernels for 0%

commit v1 on v0

--- a/solution.py
+++ b/solution.py
@@ -86,8 +86,16 @@
     queries = seg_queries[0].reshape(tok_rows, KVH, group_size, HD)
     slot_queries = mem_query.reshape(mem_rows, KVH, HD)
     row_pos = tok_index * tok_rows + jnp.arange(tok_rows)
-    kv_piece = lax.all_gather(
-        jnp.concatenate([seg_keys[0], seg_values[0]], axis=1), "tok", axis=0, tiled=True
+    kv_piece = jnp.concatenate(
+        lax.all_to_all(
+            jnp.stack(
+                [jnp.concatenate([seg_keys[0], seg_values[0]], axis=1)] * lax.axis_size("tok")
+            ),
+            "tok",
+            0,
+            0,
+        ),
+        axis=0,
     )
     piece_rows = kv_piece.shape[0]
     key_piece = kv_piece[:, :width_kv].reshape(piece_rows, KVH, HD)

time: 349 us -> 429 us (1.23)
  the two profiles are of different devices: /device:TPU:2 before, /device:TPU:4 now
where the time goes in v1:
time: 429 us; the launch traced here: 428 us
  waiting for transfers between devices  199 us (46%)
  starting transfers between devices  117 us (27%)
  matrix products  53.2 us (12%)
  local copies, waits for them, and re-layouts  32.3 us (8%)
  other arithmetic  24.2 us (6%)
    all_to_all x1, waiting for transfers between devices, shards(): lax.all_to_all(jnp.stack([jnp.concatenate([seg_keys[0], seg_values[0]], a...  177 us
    ppermute x19, starting transfers between devices, gathered(): lax.ppermute(held, axis, [(i, i ^ flip) for i in range(size)])  78.7 us
    ppermute x7, starting transfers between devices, scattered_sum(): lax.ppermute(send, axis, [(i, i ^ flip) for i in range(size)])  27.1 us
    dot_general x4, matrix products, shards(): jnp.einsum('tgjd,ugd->gjtu', queries, key_block, preferred_element_type=j...  20.6 us
    dot_general x4, matrix products, shards(): jnp.einsum('gjtu,ugd->tgjd', seg_weights, value_block, preferred_element_...  16.6 us
    reduce_sum x4, other arithmetic, softmax_step(): new_total = row_total * multiplier + jnp.sum(weights, axis=-1)  13.4 us
    ppermute x7, waiting for transfers between devices, scattered_sum(): lax.ppermute(send, axis, [(i, i ^ flip) for i in range(size)])  13 us
    all_to_all x1, starting transfers between devices, shards(): lax.all_to_all(jnp.stack([jnp.concatenate([seg_keys[0], seg_values[0]], a...  10.6 us
  transfers between devices with their start and end apart: 27, of which 11 were waited for; matrix products, arithmetic and copies ran while one was open for 7% of the time, Pallas kernels for 0%

profile of v1, /device:TPU:4, one launch (start us, length us, event | category | flops | bytes accessed | tf_op | source)
XLA Modules:
  0.0 427.8 jit_solution(13071201661787621116)
XLA Ops:
  1.8 5.2 %stack.134 = bf16[32,128,1024]{1,2,0:T(8,128)(2,1)} broadcast(bf16[128,1024]{0,1:T(8,128)(2,1)S(1)} %copy.106), dimensions={1,2} | broadcast | bytes 8650752 | tf_op jit(solution)/shard_map/stack | solution.py:91
  7.1 10.6 %all-to-all-start = ((bf16[32,128,1024]{1,2,0:T(8,128)(2,1)}), bf16[32,128,1024]{1,2,0:T(8,128)(2,1)}, u32[]{:S(2)}, u32[]{:S(2)}) async-start(bf16[32,128,1024]{1,2,0:T(8,128)(2,1)} %stack.134), calls=%async_computation | async-start | bytes 16777216 | tf_op jit(solution)/shard_map/all_to_all | solution.py:90
  25.8 176.7 %all-to-all-done = bf16[32,128,1024]{1,2,0:T(8,128)(2,1)} async-done(((bf16[32,128,1024]{1,2,0:T(8,128)(2,1)}), bf16[32,128,1024]{1,2,0:T(8,128)(2,1)}, u32[]{:S(2)}, u32[]{:S(2)}) %all-to-all-start) | async-done | bytes 8388640 | tf_op jit(solution)/shard_map/all_to_all | solution.py:90
  202.5 8.0 %copy_bitcast_fusion = bf16[4096,1024]{0,1:T(8,128)(2,1)} fusion(bf16[32,128,1024]{1,2,0:T(8,128)(2,1)} %all-to-all-done), kind=kLoop, calls=%fused_computation.1 | loop fusion | bytes 16777216 | tf_op jit(solution)/shard_map/reshape | solution.py:89
  210.5 6.1 %fusion.185 = (bf16[4096,512]{0,1:T(8,128)(2,1)}, bf16[4096,512]{0,1:T(8,128)(2,1)}) fusion(bf16[4096,1024]{0,1:T(8,128)(2,1)} %copy_bitcast_fusion), kind=kLoop, calls=%fused_computation.283 | loop fusion | bytes 16777216 | tf_op jit(solution)/shard_map/slice | solution.py:101
  219.7 3.5 fusion.80
  223.2 3.5 fusion.79
  226.9 10.7 %collective-permute-start = (f32[1,9,1024]{2,1,0:T(8,128)S(1)}, f32[1,9,1024]{2,1,0:T(8,128)S(1)}, u32[]{:S(2)}, u32[]{:S(2)}) collective-permute-start(f32[1,9,1024]{2,1,0:T(8,128)S(1)} %maximum_bitcast_fusion.1), channel_id=1, source_target_pairs={{0,384},{32,416},{64,448},{96,480},{128,256},{160,288},{192,320},{... | collective-permute-start | bytes 110600 | tf_op jit(solution)/shard_map/ppermute | solution.py:26
  239.6 4.3 collective-permute-start.2
  248.5 4.1 collective-permute-start.3
  257.7 4.9 %fusion.4 = (f32[4,4,128]{2,1,0:T(4,128)S(1)}, f32[4,1024,128,4]{2,1,3,0:T(8,128)}) fusion(pred[128,1024]{0,1:T(8,128)(4,1)S(1)} %get-tuple-element.89, bf16[1024,4,128,1]{0,2,3,1:T(8,128)(2,1)S(1)} %bitcast.625, bf16[128,4,4,128]{3,2,1,0:T(4,128)(2,1)S(1)} %reshape_squeeze.3), kind=kOutput, calls=%fused_computation.13 | convolution fusion | flops 543160320 | bytes 10100736 | tf_op jit(solution)/shard_map/tgjd,ugd->gjtu/dot_general | solution.py:155
  265.3 5.0 %collective-permute-start.6 = (bf16[1,8,1024]{2,1,0:T(8,128)(2,1)S(1)}, bf16[1,8,1024]{2,1,0:T(8,128)(2,1)S(1)}, u32[]{:S(2)}, u32[]{:S(2)}) collective-permute-start(bf16[1,8,1024]{2,1,0:T(8,128)(2,1)S(1)} %get-tuple-element.23), channel_id=1, source_target_pairs={{0,24},{1,25},{2,26},{3,27},{4,28},{5,29},{6,30},{7,31},{8,16},{9,... | collective-permute-start | bytes 49160 | tf_op jit(solution)/shard_map/ppermute | solution.py:26
  270.3 5.2 %collective-permute-start.7 = (bf16[1,8,1024]{2,1,0:T(8,128)(2,1)S(1)}, bf16[1,8,1024]{2,1,0:T(8,128)(2,1)S(1)}, u32[]{:S(2)}, u32[]{:S(2)}) collective-permute-start(bf16[1,8,1024]{2,1,0:T(8,128)(2,1)S(1)} %get-tuple-element.23), channel_id=1, source_target_pairs={{0,16},{1,17},{2,18},{3,19},{4,20},{5,21},{6,22},{7,23},{8,24},{9,... | collective-permute-start | bytes 49160 | tf_op jit(solution)/shard_map/ppermute | solution.py:26
  275.5 4.6 %collective-permute-start.8 = (bf16[1,8,1024]{2,1,0:T(8,128)(2,1)S(1)}, bf16[1,8,1024]{2,1,0:T(8,128)(2,1)S(1)}, u32[]{:S(2)}, u32[]{:S(2)}) collective-permute-start(bf16[1,8,1024]{2,1,0:T(8,128)(2,1)S(1)} %get-tuple-element.23), channel_id=1, source_target_pairs={{0,8},{1,9},{2,10},{3,11},{4,12},{5,13},{6,14},{7,15},{8,0},{9,1},... | collective-permute-start | bytes 49160 | tf_op jit(solution)/shard_map/ppermute | solution.py:26
  280.2 5.4 %fusion.3 = (f32[4,4,128]{2,1,0:T(4,128)}, f32[4,1024,128,4]{2,1,3,0:T(8,128)}) fusion(pred[128,1024]{0,1:T(8,128)(4,1)S(1)} %get-tuple-element.88, bf16[1024,4,128,1]{0,2,3,1:T(8,128)(2,1)S(1)} %bitcast.624, bf16[128,4,4,128]{3,2,1,0:T(4,128)(2,1)S(1)} %reshape_squeeze.3), kind=kOutput, calls=%fused_computation.12 | convolution fusion | flops 543160320 | bytes 10100736 | tf_op jit(solution)/shard_map/tgjd,ugd->gjtu/dot_general | solution.py:155
  285.8 10.0 %collective-permute-start.9 = (bf16[2,2,1,8,1024]{4,3,1,0,2:T(8,128)(2,1)S(1)}, bf16[2,2,1,8,1024]{4,3,1,0,2:T(8,128)(2,1)S(1)}, u32[]{:S(2)}, u32[]{:S(2)}) collective-permute-start(bf16[2,2,1,8,1024]{4,3,1,0,2:T(8,128)(2,1)S(1)} %bitcast.654), channel_id=1, source_target_pairs={{0,6},{1,7},{2,4},{3,5},{4,2},{5,3},{6,0},{7,1},{8,14},{9,15},{10,... | collective-permute-start | bytes 196616 | tf_op jit(solution)/shard_map/ppermute | solution.py:26
  300.1 5.5 %fusion.2 = (f32[4,4,128]{2,1,0:T(4,128)}, f32[4,1024,128,4]{2,1,3,0:T(8,128)}) fusion(pred[128,1024]{0,1:T(8,128)(4,1)S(1)} %get-tuple-element.90, bf16[1024,4,128,1]{0,2,3,1:T(8,128)(2,1)S(1)} %bitcast.623, bf16[128,4,4,128]{3,2,1,0:T(4,128)(2,1)S(1)} %reshape_squeeze.3), kind=kOutput, calls=%fused_computation.11 | convolution fusion | flops 543160320 | bytes 10100736 | tf_op jit(solution)/shard_map/tgjd,ugd->gjtu/dot_general | solution.py:155
  307.7 4.8 %fusion.1 = (f32[4,4,128]{2,1,0:T(4,128)S(1)}, f32[4,1024,128,4]{2,1,3,0:T(8,128)}) fusion(pred[128,1024]{0,1:T(8,128)(4,1)S(1)} %copy-done.3, bf16[1024,4,128,1]{0,2,3,1:T(8,128)(2,1)S(1)} %bitcast.622, bf16[128,4,4,128]{3,2,1,0:T(4,128)(2,1)S(1)} %reshape_squeeze.3), kind=kOutput, calls=%fused_computation.10 | convolution fusion | flops 543160320 | bytes 10100736 | tf_op jit(solution)/shard_map/tgjd,ugd->gjtu/dot_general | solution.py:155
  316.7 4.8 %fusion.11 = f32[4,4,128]{2,1,0:T(4,128)S(1)} fusion(f32[4,1024,128,4]{2,1,3,0:T(8,128)} %get-tuple-element.97, f32[4,4,128]{2,1,0:T(4,128)S(1)} %get-tuple-element.20, pred[128,1024]{0,1:T(8,128)(4,1)S(1)} %get-tuple-element.89), kind=kLoop, calls=%fused_computation.20 | loop fusion | flops 10483712 | bytes 8536064 | tf_op jit(solution)/shard_map/reduce_sum | solution.py:70
  321.6 4.6 %fusion.9 = f32[4,4,128]{2,1,0:T(4,128)S(1)} fusion(f32[4,1024,128,4]{2,1,3,0:T(8,128)} %get-tuple-element.99, f32[4,4,128]{2,1,0:T(4,128)S(1)} %get-tuple-element.21, pred[128,1024]{0,1:T(8,128)(4,1)S(1)} %get-tuple-element.88), kind=kLoop, calls=%fused_computation.18 | loop fusion | flops 10483712 | bytes 8536064 | tf_op jit(solution)/shard_map/reduce_sum | solution.py:70
  333.1 5.9 %fusion.64 = f32[128,4,4,128]{0,3,2,1:T(8,128)S(1)} fusion(bf16[1024,4,128,1]{0,2,3,1:T(8,128)(2,1)} %bitcast.639, f32[4,1024,128,4]{2,1,3,0:T(8,128)} %get-tuple-element.103, f32[4,4,128]{2,1,0:T(4,128)} %copy-done.54, pred[128,1024]{0,1:T(8,128)(4,1)} %get-tuple-element.91, f32[128,4,4]{0,2,1:T(4,128)} %get-tuple-element.83, ...), kind=kOutput, calls=%fused_computation.60 | convolution fusion | flops 547880960 | bytes 10641408 | tf_op jit(solution)/shard_map/gjtu,ugd->tgjd/dot_general | solution.py:161
  339.1 5.7 %fusion.67 = f32[128,4,4,128]{0,3,2,1:T(8,128)S(1)} fusion(f32[128,4,4,128]{0,3,2,1:T(8,128)S(1)} %fusion.64, bf16[1024,4,128,1]{0,2,3,1:T(8,128)(2,1)S(1)} %bitcast.638, f32[4,1024,128,4]{2,1,3,0:T(8,128)} %get-tuple-element.101, f32[4,4,128]{2,1,0:T(4,128)S(1)} %copy-done.23, pred[128,1024]{0,1:T(8,128)(4,1)S(1)} %get-tuple-element.90, ...), kind=kOutput, calls=%fused_computation.61 | convolution fusion | flops 547880960 | bytes 11681792 | tf_op jit(solution)/shard_map/gjtu,ugd->tgjd/dot_general | solution.py:161
  362.2 5.7 %collective-permute-start.16 = (f32[4,8,1024]{2,1,0:T(8,128)S(1)}, f32[4,8,1024]{2,1,0:T(8,128)S(1)}, u32[]{:S(2)}, u32[]{:S(2)}) collective-permute-start(f32[4,8,1024]{2,1,0:T(8,128)S(1)} %get-tuple-element.59), channel_id=1, source_target_pairs={{0,6},{1,7},{2,4},{3,5},{4,2},{5,3},{6,0},{7,1},{8,14},{9,15},{10,... | collective-permute-start | bytes 393224 | tf_op jit(solution)/shard_map/ppermute | solution.py:53
  372.4 6.9 %collective-permute-done.15 = f32[4,8,1024]{2,1,0:T(8,128)S(1)} collective-permute-done((f32[4,8,1024]{2,1,0:T(8,128)S(1)}, f32[4,8,1024]{2,1,0:T(8,128)S(1)}, u32[]{:S(2)}, u32[]{:S(2)}) %collective-permute-start.15) | collective-permute-done | bytes 131104 | tf_op jit(solution)/shard_map/ppermute | solution.py:53
  380.2 3.6 collective-permute-start.19
  383.7 5.2 %collective-permute-start.18 = (f32[1,8,1024]{2,1,0:T(8,128)S(1)}, f32[1,8,1024]{2,1,0:T(8,128)S(1)}, u32[]{:S(2)}, u32[]{:S(2)}) collective-permute-start(f32[1,8,1024]{2,1,0:T(8,128)S(1)} %get-tuple-element.78), channel_id=1, source_target_pairs={{0,16},{1,17},{2,18},{3,19},{4,20},{5,21},{6,22},{7,23},{8,24},{9,... | collective-permute-start | bytes 98312 | tf_op jit(solution)/shard_map/ppermute | solution.py:53
  388.9 5.9 %collective-permute-start.17 = (f32[1,8,1024]{2,1,0:T(8,128)S(1)}, f32[1,8,1024]{2,1,0:T(8,128)S(1)}, u32[]{:S(2)}, u32[]{:S(2)}) collective-permute-start(f32[1,8,1024]{2,1,0:T(8,128)S(1)} %get-tuple-element.76), channel_id=1, source_target_pairs={{0,8},{1,9},{2,10},{3,11},{4,12},{5,13},{6,14},{7,15},{8,0},{9,1},... | collective-permute-start | bytes 98312 | tf_op jit(solution)/shard_map/ppermute | solution.py:53
  394.8 3.8 collective-permute-done.17
  398.6 4.3 %collective-permute-start.20 = (f32[1,8,1024]{2,1,0:T(8,128)S(1)}, f32[1,8,1024]{2,1,0:T(8,128)S(1)}, u32[]{:S(2)}, u32[]{:S(2)}) collective-permute-start(f32[1,8,1024]{2,1,0:T(8,128)S(1)} %add_add_fusion), channel_id=1, source_target_pairs={{0,384},{32,416},{64,448},{96,480},{128,256},{160,288},{192,320},{... | collective-permute-start | bytes 98312 | tf_op jit(solution)/shard_map/ppermute | solution.py:26
  403.0 3.8 collective-permute-start.21
  406.7 4.1 collective-permute-start.22
  413.5 4.5 %collective-permute-start.23 = (f32[2,2,1,8,1024]{4,3,1,0,2:T(8,128)S(1)}, f32[2,2,1,8,1024]{4,3,1,0,2:T(8,128)S(1)}, u32[]{:S(2)}, u32[]{:S(2)}) collective-permute-start(f32[2,2,1,8,1024]{4,3,1,0,2:T(8,128)S(1)} %bitcast.648), channel_id=1, source_target_pairs={{0,96},{32,64},{64,32},{96,0},{128,224},{160,192},{192,160},{224,1... | collective-permute-start | bytes 393224 | tf_op jit(solution)/shard_map/ppermute | solution.py:26
  (254 shorter events, 77.8 us)
Async XLA Ops:
  0.6 215.9 %copy-start = (bf16[8,512]{1,0:T(8,128)(2,1)S(1)}, bf16[8,512]{1,0:T(8,128)(2,1)}, u32[]{:S(2)}) copy-start(bf16[8,512]{1,0:T(8,128)(2,1)} %param.14) | copy-start | bytes 24580
  7.1 195.4 %all-to-all-start = ((bf16[32,128,1024]{1,2,0:T(8,128)(2,1)}), bf16[32,128,1024]{1,2,0:T(8,128)(2,1)}, u32[]{:S(2)}, u32[]{:S(2)}) async-start(bf16[32,128,1024]{1,2,0:T(8,128)(2,1)} %stack.134), calls=%async_computation | async-start | bytes 16777216 | tf_op jit(solution)/shard_map/all_to_all | solution.py:90
  226.9 19.4 %collective-permute-start = (f32[1,9,1024]{2,1,0:T(8,128)S(1)}, f32[1,9,1024]{2,1,0:T(8,128)S(1)}, u32[]{:S(2)}, u32[]{:S(2)}) collective-permute-start(f32[1,9,1024]{2,1,0:T(8,128)S(1)} %maximum_bitcast_fusion.1), channel_id=1, source_target_pairs={{0,384},{32,416},{64,448},{96,480},{128,256},{160,288},{192,320},{... | collective-permute-start | bytes 110600 | tf_op jit(solution)/shard_map/ppermute | solution.py:26
  237.6 10.7 %collective-permute-start.1 = (f32[1,9,1024]{2,1,0:T(8,128)S(1)}, f32[1,9,1024]{2,1,0:T(8,128)S(1)}, u32[]{:S(2)}, u32[]{:S(2)}) collective-permute-start(f32[1,9,1024]{2,1,0:T(8,128)S(1)} %maximum_bitcast_fusion.1), channel_id=1, source_target_pairs={{0,256},{32,288},{64,320},{96,352},{128,384},{160,416},{192,448},{... | collective-permute-start | bytes 110600 | tf_op jit(solution)/shard_map/ppermute | solution.py:26
  239.6 8.8 %collective-permute-start.2 = (f32[1,9,1024]{2,1,0:T(8,128)S(1)}, f32[1,9,1024]{2,1,0:T(8,128)S(1)}, u32[]{:S(2)}, u32[]{:S(2)}) collective-permute-start(f32[1,9,1024]{2,1,0:T(8,128)S(1)} %maximum_bitcast_fusion.1), channel_id=1, source_target_pairs={{0,128},{32,160},{64,192},{96,224},{128,0},{160,32},{192,64},{224,... | collective-permute-start | bytes 110600 | tf_op jit(solution)/shard_map/ppermute | solution.py:26
  248.5 14.1 %collective-permute-start.3 = (f32[2,2,1,9,1024]{4,3,1,0,2:T(8,128)S(1)}, f32[2,2,1,9,1024]{4,3,1,0,2:T(8,128)S(1)}, u32[]{:S(2)}, u32[]{:S(2)}) collective-permute-start(f32[2,2,1,9,1024]{4,3,1,0,2:T(8,128)S(1)} %bitcast.640), channel_id=1, source_target_pairs={{0,96},{32,64},{64,32},{96,0},{128,224},{160,192},{192,160},{224,1... | collective-permute-start | bytes 442376 | tf_op jit(solution)/shard_map/ppermute | solution.py:26
  252.6 10.0 %collective-permute-start.4 = (f32[2,2,1,9,1024]{4,3,1,0,2:T(8,128)S(1)}, f32[2,2,1,9,1024]{4,3,1,0,2:T(8,128)S(1)}, u32[]{:S(2)}, u32[]{:S(2)}) collective-permute-start(f32[2,2,1,9,1024]{4,3,1,0,2:T(8,128)S(1)} %bitcast.641), channel_id=1, source_target_pairs={{0,64},{32,96},{64,0},{96,32},{128,192},{160,224},{192,128},{224,1... | collective-permute-start | bytes 442376 | tf_op jit(solution)/shard_map/ppermute | solution.py:26
  255.0 9.0 %collective-permute-start.5 = (f32[2,2,1,9,1024]{4,3,1,0,2:T(8,128)S(1)}, f32[2,2,1,9,1024]{4,3,1,0,2:T(8,128)S(1)}, u32[]{:S(2)}, u32[]{:S(2)}) collective-permute-start(f32[2,2,1,9,1024]{4,3,1,0,2:T(8,128)S(1)} %bitcast.642), channel_id=1, source_target_pairs={{0,32},{32,0},{64,96},{96,64},{128,160},{160,128},{192,224},{224,1... | collective-permute-start | bytes 442376 | tf_op jit(solution)/shard_map/ppermute | solution.py:26
  265.3 20.4 %collective-permute-start.6 = (bf16[1,8,1024]{2,1,0:T(8,128)(2,1)S(1)}, bf16[1,8,1024]{2,1,0:T(8,128)(2,1)S(1)}, u32[]{:S(2)}, u32[]{:S(2)}) collective-permute-start(bf16[1,8,1024]{2,1,0:T(8,128)(2,1)S(1)} %get-tuple-element.23), channel_id=1, source_target_pairs={{0,24},{1,25},{2,26},{3,27},{4,28},{5,29},{6,30},{7,31},{8,16},{9,... | collective-permute-start | bytes 49160 | tf_op jit(solution)/shard_map/ppermute | solution.py:26
  270.3 15.4 %collective-permute-start.7 = (bf16[1,8,1024]{2,1,0:T(8,128)(2,1)S(1)}, bf16[1,8,1024]{2,1,0:T(8,128)(2,1)S(1)}, u32[]{:S(2)}, u32[]{:S(2)}) collective-permute-start(bf16[1,8,1024]{2,1,0:T(8,128)(2,1)S(1)} %get-tuple-element.23), channel_id=1, source_target_pairs={{0,16},{1,17},{2,18},{3,19},{4,20},{5,21},{6,22},{7,23},{8,24},{9,... | collective-permute-start | bytes 49160 | tf_op jit(solution)/shard_map/ppermute | solution.py:26
  275.5 10.2 %collective-permute-start.8 = (bf16[1,8,1024]{2,1,0:T(8,128)(2,1)S(1)}, bf16[1,8,1024]{2,1,0:T(8,128)(2,1)S(1)}, u32[]{:S(2)}, u32[]{:S(2)}) collective-permute-start(bf16[1,8,1024]{2,1,0:T(8,128)(2,1)S(1)} %get-tuple-element.23), channel_id=1, source_target_pairs={{0,8},{1,9},{2,10},{3,11},{4,12},{5,13},{6,14},{7,15},{8,0},{9,1},... | collective-permute-start | bytes 49160 | tf_op jit(solution)/shard_map/ppermute | solution.py:26
  285.8 19.9 %collective-permute-start.9 = (bf16[2,2,1,8,1024]{4,3,1,0,2:T(8,128)(2,1)S(1)}, bf16[2,2,1,8,1024]{4,3,1,0,2:T(8,128)(2,1)S(1)}, u32[]{:S(2)}, u32[]{:S(2)}) collective-permute-start(bf16[2,2,1,8,1024]{4,3,1,0,2:T(8,128)(2,1)S(1)} %bitcast.654), channel_id=1, source_target_pairs={{0,6},{1,7},{2,4},{3,5},{4,2},{5,3},{6,0},{7,1},{8,14},{9,15},{10,... | collective-permute-start | bytes 196616 | tf_op jit(solution)/shard_map/ppermute | solution.py:26
  295.7 9.9 %collective-permute-start.10 = (bf16[2,2,1,8,1024]{4,3,1,0,2:T(8,128)(2,1)S(1)}, bf16[2,2,1,8,1024]{4,3,1,0,2:T(8,128)(2,1)S(1)}, u32[]{:S(2)}, u32[]{:S(2)}) collective-permute-start(bf16[2,2,1,8,1024]{4,3,1,0,2:T(8,128)(2,1)S(1)} %bitcast.655), channel_id=1, source_target_pairs={{0,4},{1,5},{2,6},{3,7},{4,0},{5,1},{6,2},{7,3},{8,12},{9,13},{10,... | collective-permute-start | bytes 196616 | tf_op jit(solution)/shard_map/ppermute | solution.py:26
  297.7 8.0 %collective-permute-start.11 = (bf16[2,2,1,8,1024]{4,3,1,0,2:T(8,128)(2,1)S(1)}, bf16[2,2,1,8,1024]{4,3,1,0,2:T(8,128)(2,1)S(1)}, u32[]{:S(2)}, u32[]{:S(2)}) collective-permute-start(bf16[2,2,1,8,1024]{4,3,1,0,2:T(8,128)(2,1)S(1)} %bitcast.656), channel_id=1, source_target_pairs={{0,2},{1,3},{2,0},{3,1},{4,6},{5,7},{6,4},{7,5},{8,10},{9,11},{10,... | collective-permute-start | bytes 196616 | tf_op jit(solution)/shard_map/ppermute | solution.py:26
  305.7 6.7 %collective-permute-start.12 = (bf16[2,2,2,2,1,8,1024]{6,5,3,2,1,0,4:T(8,128)(2,1)S(1)}, bf16[2,2,2,2,1,8,1024]{6,5,3,2,1,0,4:T(8,128)(2,1)S(1)}, u32[]{:S(2)}, u32[]{:S(2)}) collective-permute-start(bf16[2,2,2,2,1,8,1024]{6,5,3,2,1,0,4:T(8,128)(2,1)S(1)} %bitcast.644), channel_id=1, source_target_pairs={{0,1},{1,0},{2,3},{3,2},{4,5},{5,4},{6,7},{7,6},{8,9},{9,8},{10,11... | collective-permute-start | bytes 786440 | tf_op jit(solution)/shard_map/ppermute | solution.py:26
  352.9 74.9 %copy-start.1 = (bf16[8,512]{1,0:T(8,128)(2,1)S(1)}, bf16[8,512]{1,0:T(8,128)(2,1)}, u32[]{:S(2)}) copy-start(bf16[8,512]{1,0:T(8,128)(2,1)} %param.14) | copy-start | bytes 24580
  354.7 72.2 %copy-start.31 = (f32[1,1,1024]{2,1,0:T(1,128)S(1)}, f32[1,1,1024]{2,1,0:T(1,128)}, u32[]{:S(2)}) copy-start(f32[1,1,1024]{2,1,0:T(1,128)} %copy-done.30) | copy-start | bytes 12292
  354.8 72.2 %copy-start.33 = (f32[1,1,1024]{2,1,0:T(1,128)S(1)}, f32[1,1,1024]{2,1,0:T(1,128)}, u32[]{:S(2)}) copy-start(f32[1,1,1024]{2,1,0:T(1,128)} %copy-done.32) | copy-start | bytes 12292
  354.8 72.2 %copy-start.35 = (f32[1,1,1024]{2,1,0:T(1,128)S(1)}, f32[1,1,1024]{2,1,0:T(1,128)}, u32[]{:S(2)}) copy-start(f32[1,1,1024]{2,1,0:T(1,128)} %copy-done.34) | copy-start | bytes 12292
  358.2 3.9 collective-permute-start.13
  362.2 10.2 %collective-permute-start.16 = (f32[4,8,1024]{2,1,0:T(8,128)S(1)}, f32[4,8,1024]{2,1,0:T(8,128)S(1)}, u32[]{:S(2)}, u32[]{:S(2)}) collective-permute-start(f32[4,8,1024]{2,1,0:T(8,128)S(1)} %get-tuple-element.59), channel_id=1, source_target_pairs={{0,6},{1,7},{2,4},{3,5},{4,2},{5,3},{6,0},{7,1},{8,14},{9,15},{10,... | collective-permute-start | bytes 393224 | tf_op jit(solution)/shard_map/ppermute | solution.py:53
  368.0 11.4 %collective-permute-start.15 = (f32[4,8,1024]{2,1,0:T(8,128)S(1)}, f32[4,8,1024]{2,1,0:T(8,128)S(1)}, u32[]{:S(2)}, u32[]{:S(2)}) collective-permute-start(f32[4,8,1024]{2,1,0:T(8,128)S(1)} %get-tuple-element.60), channel_id=1, source_target_pairs={{0,4},{1,5},{2,6},{3,7},{4,0},{5,1},{6,2},{7,3},{8,12},{9,13},{10,... | collective-permute-start | bytes 393224 | tf_op jit(solution)/shard_map/ppermute | solution.py:53
  369.9 10.2 %collective-permute-start.14 = (f32[4,8,1024]{2,1,0:T(8,128)S(1)}, f32[4,8,1024]{2,1,0:T(8,128)S(1)}, u32[]{:S(2)}, u32[]{:S(2)}) collective-permute-start(f32[4,8,1024]{2,1,0:T(8,128)S(1)} %get-tuple-element.58), channel_id=1, source_target_pairs={{0,2},{1,3},{2,0},{3,1},{4,6},{5,7},{6,4},{7,5},{8,10},{9,11},{10,... | collective-permute-start | bytes 393224 | tf_op jit(solution)/shard_map/ppermute | solution.py:53
  380.2 14.7 %collective-permute-start.19 = (f32[1,8,1024]{2,1,0:T(8,128)S(1)}, f32[1,8,1024]{2,1,0:T(8,128)S(1)}, u32[]{:S(2)}, u32[]{:S(2)}) collective-permute-start(f32[1,8,1024]{2,1,0:T(8,128)S(1)} %get-tuple-element.77), channel_id=1, source_target_pairs={{0,24},{1,25},{2,26},{3,27},{4,28},{5,29},{6,30},{7,31},{8,16},{9,... | collective-permute-start | bytes 98312 | tf_op jit(solution)/shard_map/ppermute | solution.py:53
  383.7 11.1 %collective-permute-start.18 = (f32[1,8,1024]{2,1,0:T(8,128)S(1)}, f32[1,8,1024]{2,1,0:T(8,128)S(1)}, u32[]{:S(2)}, u32[]{:S(2)}) collective-permute-start(f32[1,8,1024]{2,1,0:T(8,128)S(1)} %get-tuple-element.78), channel_id=1, source_target_pairs={{0,16},{1,17},{2,18},{3,19},{4,20},{5,21},{6,22},{7,23},{8,24},{9,... | collective-permute-start | bytes 98312 | tf_op jit(solution)/shard_map/ppermute | solution.py:53
  388.9 9.7 %collective-permute-start.17 = (f32[1,8,1024]{2,1,0:T(8,128)S(1)}, f32[1,8,1024]{2,1,0:T(8,128)S(1)}, u32[]{:S(2)}, u32[]{:S(2)}) collective-permute-start(f32[1,8,1024]{2,1,0:T(8,128)S(1)} %get-tuple-element.76), channel_id=1, source_target_pairs={{0,8},{1,9},{2,10},{3,11},{4,12},{5,13},{6,14},{7,15},{8,0},{9,1},... | collective-permute-start | bytes 98312 | tf_op jit(solution)/shard_map/ppermute | solution.py:53
  398.6 12.2 %collective-permute-start.20 = (f32[1,8,1024]{2,1,0:T(8,128)S(1)}, f32[1,8,1024]{2,1,0:T(8,128)S(1)}, u32[]{:S(2)}, u32[]{:S(2)}) collective-permute-start(f32[1,8,1024]{2,1,0:T(8,128)S(1)} %add_add_fusion), channel_id=1, source_target_pairs={{0,384},{32,416},{64,448},{96,480},{128,256},{160,288},{192,320},{... | collective-permute-start | bytes 98312 | tf_op jit(solution)/shard_map/ppermute | solution.py:26
  403.0 9.7 %collective-permute-start.21 = (f32[1,8,1024]{2,1,0:T(8,128)S(1)}, f32[1,8,1024]{2,1,0:T(8,128)S(1)}, u32[]{:S(2)}, u32[]{:S(2)}) collective-permute-start(f32[1,8,1024]{2,1,0:T(8,128)S(1)} %add_add_fusion), channel_id=1, source_target_pairs={{0,256},{32,288},{64,320},{96,352},{128,384},{160,416},{192,448},{... | collective-permute-start | bytes 98312 | tf_op jit(solution)/shard_map/ppermute | solution.py:26
  406.7 6.7 %collective-permute-start.22 = (f32[1,8,1024]{2,1,0:T(8,128)S(1)}, f32[1,8,1024]{2,1,0:T(8,128)S(1)}, u32[]{:S(2)}, u32[]{:S(2)}) collective-permute-start(f32[1,8,1024]{2,1,0:T(8,128)S(1)} %add_add_fusion), channel_id=1, source_target_pairs={{0,128},{32,160},{64,192},{96,224},{128,0},{160,32},{192,64},{224,... | collective-permute-start | bytes 98312 | tf_op jit(solution)/shard_map/ppermute | solution.py:26
  413.5 10.4 %collective-permute-start.23 = (f32[2,2,1,8,1024]{4,3,1,0,2:T(8,128)S(1)}, f32[2,2,1,8,1024]{4,3,1,0,2:T(8,128)S(1)}, u32[]{:S(2)}, u32[]{:S(2)}) collective-permute-start(f32[2,2,1,8,1024]{4,3,1,0,2:T(8,128)S(1)} %bitcast.648), channel_id=1, source_target_pairs={{0,96},{32,64},{64,32},{96,0},{128,224},{160,192},{192,160},{224,1... | collective-permute-start | bytes 393224 | tf_op jit(solution)/shard_map/ppermute | solution.py:26
  417.9 6.9 %collective-permute-start.24 = (f32[2,2,1,8,1024]{4,3,1,0,2:T(8,128)S(1)}, f32[2,2,1,8,1024]{4,3,1,0,2:T(8,128)S(1)}, u32[]{:S(2)}, u32[]{:S(2)}) collective-permute-start(f32[2,2,1,8,1024]{4,3,1,0,2:T(8,128)S(1)} %bitcast.649), channel_id=1, source_target_pairs={{0,64},{32,96},{64,0},{96,32},{128,192},{160,224},{192,128},{224,1... | collective-permute-start | bytes 393224 | tf_op jit(solution)/shard_map/ppermute | solution.py:26
  419.9 6.9 %collective-permute-start.25 = (f32[2,2,1,8,1024]{4,3,1,0,2:T(8,128)S(1)}, f32[2,2,1,8,1024]{4,3,1,0,2:T(8,128)S(1)}, u32[]{:S(2)}, u32[]{:S(2)}) collective-permute-start(f32[2,2,1,8,1024]{4,3,1,0,2:T(8,128)S(1)} %bitcast.650), channel_id=1, source_target_pairs={{0,32},{32,0},{64,96},{96,64},{128,160},{160,128},{192,224},{224,1... | collective-permute-start | bytes 393224 | tf_op jit(solution)/shard_map/ppermute | solution.py:26
  (67 other events, 1554.7 us)
